TPU v7x, 128 devices: a whole 4x4x4 slice. The times are simulated.
128 devices in a mesh: seq: 16 (over z, x), exp: 8 (over y, core).
Axes of the slice: x: 4, y: 4, z: 4, core: 2. Of those that a mesh axis runs over, the one named last changes fastest.
Arguments:
- residual_in: bfloat16 [8, 4096, 2048], P('exp', 'seq'), may hold values from -6 to 6
- query_matrix: bfloat16 [8, 4096, 2048], P('exp', 'seq'), may hold values from -6 to 6
- key_vectors: bfloat16 [8, 4096, 2048], P('exp', 'seq'), may hold values from -6 to 6
- value_vectors: bfloat16 [8, 4096, 2048], P('exp', 'seq'), may hold values from -6 to 6
- head_gain: float32 [2048], replicated, may hold values from 0.5 to 1.5
- norm_gain: float32 [2048], replicated, may hold values from 0.5 to 1.5
- expert_ids: int32 [8, 4096, 4], P('exp', 'seq'), may hold values from 0 to 7, all different within a row; in each aligned block of 256 rows (0 to 255, 256 to 511, ..., all dimensions but the last counted through in order) at most 192 rows name the same one
- gate_probs: float32 [8, 4096, 4], P('exp', 'seq'), may hold values from 0.25 to 1
- w_gate: bfloat16 [8, 2048, 1408], P('exp'), may hold values from -0.125 to 0.125
- w_up: bfloat16 [8, 2048, 1408], P('exp'), may hold values from -0.125 to 0.125
- w_down: bfloat16 [8, 1408, 2048], P('exp'), may hold values from -0.15625 to 0.15625
Outputs:
- layer_out: bfloat16 [8, 4096, 2048], P('exp', 'seq')
Inputs may be any that keep to these rules, and one draw needn't show every extreme that they name: `expert_ids`: the 4 experts of one position differ; among the 256 positions of one device, no expert is named by more than 192 routes.
All inputs are finite; a program needn't handle non-finite values.
Results may differ from a plain program's by a relative error of at most 0.013.
Values may be sent and summed in bfloat16 or wider, within the bound.
No kernel may reach another device: no remote copies, remote signals or barrier semaphores. Data moves between devices by JAX's collectives and lax.ppermute only.
A program may use at most 128 MiB of HBM per device.

v0:
```python
import jax
import jax.numpy as jnp
from jax import lax
from jax.sharding import PartitionSpec as P

D = 2048
HEADS = 16
HD = 128
TOP = 4
EXPERTS = 8
CAP = 192


def on_device(
    residual_in,
    query_matrix,
    key_vectors,
    value_vectors,
    head_gain,
    norm_gain,
    expert_ids,
    gate_probs,
    w_gate,
    w_up,
    w_down,
):
    positions = residual_in.shape[1]
    queries = query_matrix[0].reshape(positions, HEADS, HD)
    key_rows = key_vectors[0].reshape(positions, HEADS, HD)
    value_rows = value_vectors[0].reshape(positions, HEADS, HD)
    state = jnp.einsum("thd,the->hde", key_rows, value_rows, preferred_element_type=jnp.float32)
    my_index = lax.axis_index("seq")
    piece = lax.all_gather(state[None], "seq", axis=0, tiled=True)
    owners = jnp.arange(piece.shape[0], dtype=jnp.int32)
    earlier = owners < my_index
    prefix = jnp.sum(jnp.where(earlier[:, None, None, None], piece, 0.0), axis=0)
    causal = jnp.tril(jnp.ones((positions, positions), dtype=bool))
    scores = jnp.einsum("thd,uhd->htu", queries, key_rows, preferred_element_type=jnp.float32)
    weights = jnp.where(causal[None], scores, 0.0).astype(jnp.bfloat16)
    inner = jnp.einsum("htu,uhd->thd", weights, value_rows, preferred_element_type=jnp.float32)
    outer_product = jnp.einsum(
        "thd,hde->the", queries, prefix.astype(jnp.bfloat16), preferred_element_type=jnp.float32
    )
    mixed = inner + outer_product
    mean_square = jnp.mean(mixed * mixed, axis=-1, keepdims=True)
    attn = (mixed * lax.rsqrt(mean_square + 1e-06)).reshape(positions, D) * head_gain
    resid_float = (
        (residual_in[0].astype(jnp.float32) + attn).astype(jnp.bfloat16).astype(jnp.float32)
    )
    row_square = jnp.mean(resid_float * resid_float, axis=-1, keepdims=True)
    normed = (resid_float * lax.rsqrt(row_square + 1e-06) * norm_gain).astype(jnp.bfloat16)
    route_ids = expert_ids[0].reshape(-1)
    route_gates = gate_probs[0]
    expert_indicator = (route_ids[:, None] == jnp.arange(EXPERTS, dtype=jnp.int32)[None, :]).astype(
        jnp.int32
    )
    slots = jnp.sum(
        (jnp.cumsum(expert_indicator, axis=0) - expert_indicator) * expert_indicator, axis=1
    )
    target = route_ids * CAP + slots
    token_of = jnp.arange(positions * TOP, dtype=jnp.int32) // TOP
    outgoing = (
        jnp.zeros((EXPERTS * CAP, D), jnp.bfloat16)
        .at[target]
        .set(normed[token_of])
        .reshape(EXPERTS, CAP, D)
    )
    local_count = w_gate.shape[0]
    groups = EXPERTS // local_count
    block = lax.all_to_all(outgoing, "exp", split_axis=0, concat_axis=0, tiled=True)
    count = block.shape[1]
    grouped = block.reshape(groups, local_count, count, D)
    gate_part = jnp.einsum("gend,edf->genf", grouped, w_gate, preferred_element_type=jnp.float32)
    up_part = jnp.einsum("gend,edf->genf", grouped, w_up, preferred_element_type=jnp.float32)
    hidden = (jax.nn.silu(gate_part) * up_part).astype(jnp.bfloat16)
    result = jnp.einsum("genf,efd->gend", hidden, w_down, preferred_element_type=jnp.float32)
    result = result.astype(jnp.bfloat16).reshape(EXPERTS, count, D)
    returned = lax.all_to_all(result, "exp", split_axis=0, concat_axis=0, tiled=True)
    picked = returned.reshape(EXPERTS * CAP, D)[target].reshape(positions, TOP, D)
    combined = jnp.sum(picked.astype(jnp.float32) * route_gates[:, :, None], axis=1)
    return (resid_float + combined).astype(jnp.bfloat16)[None]


def solution(mesh):
    in_specs = (
        P("exp", "seq", None),
        P("exp", "seq", None),
        P("exp", "seq", None),
        P("exp", "seq", None),
        P(),
        P(),
        P("exp", "seq", None),
        P("exp", "seq", None),
        P("exp", None, None),
        P("exp", None, None),
        P("exp", None, None),
    )
    out_specs = P("exp", "seq", None)
    return jax.shard_map(
        on_device, mesh=mesh, in_specs=in_specs, out_specs=out_specs, check_vma=False
    )
```

profile of v0, /device:TPU:1, one launch (start us, length us, event | category | flops | bytes accessed | tf_op | source)
XLA Modules:
  0.0 405.5 jit_solution(9483026792404834334)
XLA Ops:
  6.5 0.0 copy-start.5
  6.5 0.0 all-gather.3.cloned.1.call-start
  6.5 1.5 copy.43
  8.0 1.5 copy.45
  9.5 1.4 fusion.30
  10.9 0.0 all-gather.3.cloned.1.call-update
  11.0 0.0 copy-done.5
  11.0 0.1 copy.38
  11.1 0.1 eq.29
  11.2 0.1 eq.25
  11.4 1.5 copy.44
  12.8 2.3 reduce-window.6
  15.1 0.3 slice_reduce_fusion
  15.4 0.2 reduce-window.9
  15.5 0.1 copy.37
  15.7 0.1 mul.92
  15.9 0.1 add_bitcast_fusion
  16.0 2.7 fusion.28
  18.7 106.7 %all-gather.3.cloned.1.call-done = f32[256,128,128]{2,1,0:T(8,128)} async-done(((f32[16,128,128]{2,1,0:T(8,128)}), f32[256,128,128]{2,1,0:T(8,128)}) %all-gather.3.cloned.1.call-update) | async-done | bytes 16777232 | tf_op jit(solution)/shard_map/all_gather | solution.py:33
  125.5 0.0 copy-start.3
  125.5 8.9 %select_reduce_fusion = bf16[16,128,128]{2,1,0:T(8,128)(2,1)} fusion(f32[16,16,128,128]{3,2,1,0:T(8,128)} %bitcast.112, pred[16]{0:T(512)(128)(4,1)S(1)} %iota_compare_fusion.3), kind=kLoop, calls=%fused_computation.3 | loop fusion | flops 8126464 | bytes 17301520 | tf_op jit(solution)/shard_map/reduce_sum | solution.py:36
  134.4 0.0 copy-done.3
  134.4 1.6 multiply_reduce_fusion.1
  136.1 0.0 copy-start.2
  136.1 0.0 copy-start.4
  136.1 0.2 broadcast_multiply_fusion
  136.3 0.0 copy-start.6
  136.3 1.9 copy.40
  138.2 0.0 copy-done.2
  138.2 0.0 copy-done.4
  138.2 2.1 fusion.24
  140.3 0.0 copy-done.6
  140.3 1.3 fusion.26
  141.6 23.1 %scatter_custom_fusion = bf16[1536,2048]{1,0:T(8,128)(2,1)} fusion(s32[1024]{0:T(1024)S(1)} %bitcast.122, bf16[256,2048]{1,0:T(8,128)(2,1)} %fusion.26, s32[1024]{0:T(1024)S(1)} %broadcast_clamp_fusion.1, bf16[]{:T(256)} %constant.44.clone.1), kind=kCustom, calls=%fused_computation.20 | custom fusion | bytes 6291968 | tf_op jit(solution)/shard_map/scatter | solution.py:65
  164.8 76.4 %all_to_all.10 = bf16[8,192,2048]{2,1,0:T(8,128)(2,1)S(1)} all-to-all(bf16[8,192,2048]{2,1,0:T(8,128)(2,1)} %bitcast.109), channel_id=1, replica_groups=mesh['seq'=16,'exp'=8] {'exp'}, dimensions={0} | all-to-all | bytes 12582912 | tf_op jit(solution)/shard_map/all_to_all | solution.py:70
  241.2 0.0 copy-start.1
  241.2 2.6 copy-done.1
  243.7 13.4 %fusion.6 = f32[8,192,1408]{2,1,0:T(8,128)} fusion(bf16[8,192,2048]{2,1,0:T(8,128)(2,1)S(1)} %all_to_all.10, bf16[1,2048,1408]{2,1,0:T(8,128)(2,1)} %param.20), kind=kOutput, calls=%fused_computation.14 | convolution fusion | flops 8858370048 | bytes 20709376 | tf_op jit(solution)/shard_map/gend,edf->genf/dot_general | solution.py:74
  257.1 28.7 %fusion.9 = bf16[8,192,2048]{2,1,0:T(8,128)(2,1)} fusion(bf16[1,1408,2048]{2,1,0:T(8,128)(2,1)} %param.21, f32[8,192,1408]{2,1,0:T(8,128)} %fusion.6, bf16[8,192,2048]{2,1,0:T(8,128)(2,1)} %copy-done.1, bf16[1,2048,1408]{2,1,0:T(8,128)(2,1)} %param.19), kind=kOutput, calls=%fused_computation.17 | convolution fusion | flops 17732861952 | bytes 32768000 | tf_op jit(solution)/shard_map/genf,efd->gend/dot_general | solution.py:76
  285.8 0.0 copy-start.7
  285.8 6.0 %all-to-all-start.1 = ((bf16[8,192,2048]{2,1,0:T(8,128)(2,1)}), bf16[8,192,2048]{2,1,0:T(8,128)(2,1)}, u32[]{:S(2)}, u32[]{:S(2)}) async-start(bf16[8,192,2048]{2,1,0:T(8,128)(2,1)} %fusion.9), calls=%async_computation.1 | async-start | bytes 12582912 | tf_op jit(solution)/shard_map/all_to_all | solution.py:78
  291.9 0.0 copy-done.7
  291.9 0.1 copy.41
  292.0 1.8 copy.36
  293.8 69.2 %all-to-all-done.1 = bf16[8,192,2048]{2,1,0:T(8,128)(2,1)} async-done(((bf16[8,192,2048]{2,1,0:T(8,128)(2,1)}), bf16[8,192,2048]{2,1,0:T(8,128)(2,1)}, u32[]{:S(2)}, u32[]{:S(2)}) %all-to-all-start.1) | async-done | bytes 6291488 | tf_op jit(solution)/shard_map/all_to_all | solution.py:78
  363.1 12.4 %gather_fusion = bf16[1024,2048]{1,0:T(8,128)(2,1)} fusion(bf16[1536,2048]{1,0:T(8,128)(2,1)} %bitcast.26, s32[1024]{0:T(1024)S(1)} %broadcast_clamp_fusion), kind=kCustom, calls=%fused_computation.1 | custom fusion | bytes 8392704 | tf_op jit(solution)/shard_map/gather | solution.py:79
  375.5 8.3 %reshape.198 = f32[256,4,2048]{2,1,0:T(4,128)} reshape(bf16[1024,2048]{1,0:T(8,128)(2,1)} %gather_fusion) | data formatting | bytes 12582912 | tf_op jit(solution)/shard_map/convert_element_type | solution.py:80
  383.8 0.0 copy-start
  383.8 11.5 %multiply_reduce_fusion = f32[256,2048]{1,0:T(8,128)} fusion(f32[256,4,2048]{2,1,0:T(4,128)} %reshape.198, f32[256,4]{1,0:T(8,128)S(1)} %copy.41), kind=kLoop, calls=%fused_computation.11 | loop fusion | flops 3670016 | bytes 10489856 | tf_op jit(solution)/shard_map/reduce_sum | solution.py:80
  395.3 0.0 copy-done
  395.3 3.1 fusion.27
  (11 shorter events, 0.1 us)
Async XLA Ops:
  6.5 4.4 %copy-start.5 = (s32[1,256,4]{1,2,0:T(4,128)S(1)}, s32[1,256,4]{1,2,0:T(4,128)}, u32[]{:S(2)}) copy-start(s32[1,256,4]{1,2,0:T(4,128)} %param.17) | copy-start | bytes 12292
  6.5 119.0 %all-gather.3.cloned.1.call-start = ((), (), s32[]{:S(2)}) async-start(), calls=%async_computation.2 | async-start | bytes 17825792 | tf_op jit(solution)/shard_map/all_gather | solution.py:33
  125.5 9.0 %copy-start.3 = (f32[16,256,128]{1,2,0:T(8,128)S(1)}, f32[16,256,128]{1,2,0:T(8,128)}, u32[]{:S(2)}) copy-start(f32[16,256,128]{1,2,0:T(8,128)} %fusion.28) | copy-start | bytes 6291460
  136.1 2.1 copy-start.2
  136.1 2.1 copy-start.4
  136.3 4.0 copy-start.6
  241.2 2.6 copy-start.1
  285.8 6.0 %copy-start.7 = (f32[1,256,4]{1,2,0:T(4,128)S(1)}, f32[1,256,4]{1,2,0:T(4,128)}, u32[]{:S(2)}) copy-start(f32[1,256,4]{1,2,0:T(4,128)} %param.18) | copy-start | bytes 12292
  285.8 77.3 %all-to-all-start.1 = ((bf16[8,192,2048]{2,1,0:T(8,128)(2,1)}), bf16[8,192,2048]{2,1,0:T(8,128)(2,1)}, u32[]{:S(2)}, u32[]{:S(2)}) async-start(bf16[8,192,2048]{2,1,0:T(8,128)(2,1)} %fusion.9), calls=%async_computation.1 | async-start | bytes 12582912 | tf_op jit(solution)/shard_map/all_to_all | solution.py:78
  383.8 11.5 %copy-start = (f32[1,256,2048]{2,1,0:T(8,128)S(1)}, f32[1,256,2048]{2,1,0:T(8,128)}, u32[]{:S(2)}) copy-start(f32[1,256,2048]{2,1,0:T(8,128)} %copy.36) | copy-start | bytes 6291460
Sparse Core Ops, SparseCore 0:
  11.1 114.3 all-gather.2
where the time goes:
time: 412 us; the launch traced here: 405 us
  waiting for transfers between devices  176 us (43%)
  blocking collectives  76.4 us (19%)
  local copies, waits for them, and re-layouts  55.6 us (13%)
  matrix products  47.8 us (12%)
  other arithmetic  29.7 us (7%)
  between operations  13.8 us (3%)
  starting transfers between devices  6.04 us (1%)
    all_gather x1, waiting for transfers between devices, on_device(): piece = lax.all_gather(state[None], 'seq', axis=0, tiled=True)  107 us
    all_to_all x1, blocking collectives, on_device(): lax.all_to_all(outgoing, 'exp', split_axis=0, concat_axis=0, tiled=True)  76.4 us
    all_to_all x1, waiting for transfers between devices, on_device(): lax.all_to_all(result, 'exp', split_axis=0, concat_axis=0, tiled=True)  69.2 us
    dot_general x1, matrix products, on_device(): jnp.einsum('genf,efd->gend', hidden, w_down, preferred_element_type=jnp.f...  28.7 us
    scatter x1, local copies, waits for them, and re-layouts, on_device(): outgoing = jnp.zeros((EXPERTS * CAP, D), jnp.bfloat16).at[target].set(nor...  23.1 us
    dot_general x1, matrix products, on_device(): jnp.einsum('gend,edf->genf', grouped, w_up, preferred_element_type=jnp.fl...  13.4 us
    gather x1, local copies, waits for them, and re-layouts, on_device(): returned.reshape(EXPERTS * CAP, D)[target].reshape(positions, TOP, D)  12.4 us
    reduce_sum x1, other arithmetic, on_device(): jnp.sum(picked.astype(jnp.float32) * route_gates[:, :, None], axis=1)  11.5 us
  transfers between devices with their start and end apart: 2, of which 2 were waited for; matrix products, arithmetic and copies ran while one was open for 2% of the time, Pallas kernels for 0%

commit v1 on v0

--- a/solution.py
+++ b/solution.py
@@ -30,7 +30,26 @@
     value_rows = value_vectors[0].reshape(positions, HEADS, HD)
     state = jnp.einsum("thd,the->hde", key_rows, value_rows, preferred_element_type=jnp.float32)
     my_index = lax.axis_index("seq")
-    piece = lax.all_gather(state[None], "seq", axis=0, tiled=True)
+    devices, index, width = (lax.axis_size("seq"), lax.axis_index("seq"), state[None].shape[0])
+    right = [(i, (i + 1) % devices) for i in range(devices)]
+    left = [(i, (i - 1) % devices) for i in range(devices)]
+    out = jnp.zeros(
+        (*state[None].shape[:0], devices * width, *state[None].shape[0 + 1 :]), state[None].dtype
+    )
+    out = lax.dynamic_update_slice_in_dim(out, state[None], index * width, axis=0)
+    from_left = from_right = state[None]
+    middle = devices // 2
+    for hop in range(1, middle + 1):
+        from_left = lax.ppermute(from_left, "seq", right)
+        out = lax.dynamic_update_slice_in_dim(
+            out, from_left, (index - hop) % devices * width, axis=0
+        )
+        if hop < devices - middle:
+            from_right = lax.ppermute(from_right, "seq", left)
+            out = lax.dynamic_update_slice_in_dim(
+                out, from_right, (index + hop) % devices * width, axis=0
+            )
+    piece = out
     owners = jnp.arange(piece.shape[0], dtype=jnp.int32)
     earlier = owners < my_index
     prefix = jnp.sum(jnp.where(earlier[:, None, None, None], piece, 0.0), axis=0)

time: 412 us -> 502 us (1.22)
  starting transfers between devices: 6.04 us -> 41.8 us
  local copies, waits for them, and re-layouts: 55.6 us -> 91.1 us
  waiting for transfers between devices: 176 us -> 199 us
  between operations: 13.8 us -> 0.8 us
  blocking collectives: 76.4 us -> 82.9 us
    ppermute x0 -> x15, waiting for transfers between devices: none -> 130 us  [the longest x8 130 us: on_device(): from_left = lax.ppermute(from_left, 'seq', right)]
    all_gather x1 -> x0, waiting for transfers between devices: 107 us -> none  [on_device(): piece = lax.all_gather(state[None], 'seq', axis=0, tiled=True)]
    ppermute x0 -> x15, starting transfers between devices: none -> 35.8 us  [the longest x7 33.5 us: on_device(): from_right = lax.ppermute(from_right, 'seq', left)]
    dynamic_update_slice x0 -> x15, local copies, waits for them, and re-layouts: none -> 27.4 us  [the longest x8 15 us: on_device(): lax.dynamic_update_slice_in_dim(out, from_left, (index - hop) % devices *...]
    broadcast_in_dim x0 -> x1, local copies, waits for them, and re-layouts: none -> 7.87 us  [on_device(): jnp.zeros((*state[None].shape[:0], devices * width, *state[None].shape[0...]
    all_to_all x1, blocking collectives: 76.4 us -> 82.9 us  [on_device(): lax.all_to_all(outgoing, 'exp', split_axis=0, concat_axis=0, tiled=True)]
  transfers between devices with their start and end apart: 2 -> 16, of which waited for: 2 -> 9; matrix products, arithmetic and copies ran while one was open for 2% -> 7% of each run, Pallas kernels for 0% -> 0%
where the time goes in v1:
time: 502 us; the launch traced here: 493 us
  waiting for transfers between devices  199 us (40%)
  local copies, waits for them, and re-layouts  91.1 us (18%)
  blocking collectives  82.9 us (17%)
  matrix products  48.5 us (10%)
  starting transfers between devices  41.8 us (8%)
  other arithmetic  28.7 us (6%)
    ppermute x8, waiting for transfers between devices, on_device(): from_left = lax.ppermute(from_left, 'seq', right)  130 us
    all_to_all x1, blocking collectives, on_device(): lax.all_to_all(outgoing, 'exp', split_axis=0, concat_axis=0, tiled=True)  82.9 us
    all_to_all x1, waiting for transfers between devices, on_device(): lax.all_to_all(result, 'exp', split_axis=0, concat_axis=0, tiled=True)  69.2 us
    ppermute x7, starting transfers between devices, on_device(): from_right = lax.ppermute(from_right, 'seq', left)  33.5 us
    dot_general x1, matrix products, on_device(): jnp.einsum('genf,efd->gend', hidden, w_down, preferred_element_type=jnp.f...  28.7 us
    scatter x1, local copies, waits for them, and re-layouts, on_device(): outgoing = jnp.zeros((EXPERTS * CAP, D), jnp.bfloat16).at[target].set(nor...  23.3 us
    dynamic_update_slice x8, local copies, waits for them, and re-layouts, on_device(): lax.dynamic_update_slice_in_dim(out, from_left, (index - hop) % devices *...  15 us
    dot_general x1, matrix products, on_device(): jnp.einsum('gend,edf->genf', grouped, w_up, preferred_element_type=jnp.fl...  13.4 us
  transfers between devices with their start and end apart: 16, of which 9 were waited for; matrix products, arithmetic and copies ran while one was open for 7% of the time, Pallas kernels for 0%

profile of v1, /device:TPU:1, one launch (start us, length us, event | category | flops | bytes accessed | tf_op | source)
XLA Modules:
  0.0 493.1 jit_solution(12730358671247627213)
XLA Ops:
  0.0 1.5 copy.43
  1.5 1.5 copy.45
  3.0 7.9 %broadcast_in_dim.33 = f32[16,16,128,128]{3,2,1,0:T(8,128)} broadcast(f32[]{:T(128)} %constant.121.clone.1), dimensions={} | broadcast | bytes 16777220 | tf_op jit(solution)/shard_map/broadcast_in_dim | solution.py:36
  10.8 1.4 constant_dynamic-update-slice_fusion.15
  12.3 2.1 collective-permute-start
  14.3 4.7 collective-permute-start.1
  19.0 22.9 %collective-permute-done = f32[1,16,128,128]{3,2,1,0:T(8,128)S(1)} collective-permute-done((f32[1,16,128,128]{3,2,1,0:T(8,128)S(1)}, f32[1,16,128,128]{3,2,1,0:T(8,128)S(1)}, u32[]{:S(2)}, u32[]{:S(2)}) %collective-permute-start) | collective-permute-done | bytes 1048608 | tf_op jit(solution)/shard_map/ppermute | solution.py:43
  41.9 4.8 collective-permute-start.3
  46.7 22.0 %collective-permute-done.2 = f32[1,16,128,128]{3,2,1,0:T(8,128)S(1)} collective-permute-done((f32[1,16,128,128]{3,2,1,0:T(8,128)S(1)}, f32[1,16,128,128]{3,2,1,0:T(8,128)S(1)}, u32[]{:S(2)}, u32[]{:S(2)}) %collective-permute-start.2) | collective-permute-done | bytes 1048608 | tf_op jit(solution)/shard_map/ppermute | solution.py:43
  68.7 4.8 collective-permute-start.5
  73.5 21.1 %collective-permute-done.4 = f32[1,16,128,128]{3,2,1,0:T(8,128)S(1)} collective-permute-done((f32[1,16,128,128]{3,2,1,0:T(8,128)S(1)}, f32[1,16,128,128]{3,2,1,0:T(8,128)S(1)}, u32[]{:S(2)}, u32[]{:S(2)}) %collective-permute-start.4) | collective-permute-done | bytes 1048608 | tf_op jit(solution)/shard_map/ppermute | solution.py:43
  94.6 4.8 collective-permute-start.7
  99.4 20.4 %collective-permute-done.6 = f32[1,16,128,128]{3,2,1,0:T(8,128)} collective-permute-done((f32[1,16,128,128]{3,2,1,0:T(8,128)S(1)}, f32[1,16,128,128]{3,2,1,0:T(8,128)}, u32[]{:S(2)}, u32[]{:S(2)}) %collective-permute-start.6) | collective-permute-done | bytes 1048608 | tf_op jit(solution)/shard_map/ppermute | solution.py:43
  119.9 0.1 copy.38
  120.0 0.1 eq.45
  120.2 2.3 reduce-window.6
  122.5 4.8 collective-permute-start.9
  127.3 0.3 slice_reduce_fusion
  127.7 1.5 copy.44
  129.2 0.2 reduce-window.9
  129.3 0.1 copy.37
  129.5 0.1 mul.92
  129.6 14.8 %collective-permute-done.8 = f32[1,16,128,128]{3,2,1,0:T(8,128)} collective-permute-done((f32[1,16,128,128]{3,2,1,0:T(8,128)}, f32[1,16,128,128]{3,2,1,0:T(8,128)}, u32[]{:S(2)}, u32[]{:S(2)}) %collective-permute-start.8) | collective-permute-done | bytes 1048608 | tf_op jit(solution)/shard_map/ppermute | solution.py:43
  144.5 2.7 fusion.28
  147.2 4.8 collective-permute-start.11
  152.3 15.8 %collective-permute-done.10 = f32[1,16,128,128]{3,2,1,0:T(8,128)} collective-permute-done((f32[1,16,128,128]{3,2,1,0:T(8,128)}, f32[1,16,128,128]{3,2,1,0:T(8,128)}, u32[]{:S(2)}, u32[]{:S(2)}) %collective-permute-start.10) | collective-permute-done | bytes 1048608 | tf_op jit(solution)/shard_map/ppermute | solution.py:43
  168.1 2.3 constant_dynamic-update-slice_fusion.14
  170.4 2.3 constant_dynamic-update-slice_fusion.13
  172.7 2.3 constant_dynamic-update-slice_fusion.12
  175.0 1.0 constant_dynamic-update-slice_fusion.11
  176.1 1.1 constant_dynamic-update-slice_fusion.10
  177.2 4.9 collective-permute-start.13
  182.0 1.1 constant_dynamic-update-slice_fusion.9
  183.1 7.7 %collective-permute-done.12 = f32[1,16,128,128]{3,2,1,0:T(8,128)S(1)} collective-permute-done((f32[1,16,128,128]{3,2,1,0:T(8,128)}, f32[1,16,128,128]{3,2,1,0:T(8,128)S(1)}, u32[]{:S(2)}, u32[]{:S(2)}) %collective-permute-start.12) | collective-permute-done | bytes 1048608 | tf_op jit(solution)/shard_map/ppermute | solution.py:43
  190.8 0.2 collective-permute-start.14
  191.0 2.4 constant_dynamic-update-slice_fusion.8
  193.4 2.3 constant_dynamic-update-slice_fusion.7
  195.6 2.3 constant_dynamic-update-slice_fusion.6
  198.0 2.3 constant_dynamic-update-slice_fusion.5
  200.3 2.3 constant_dynamic-update-slice_fusion.4
  202.6 2.3 constant_dynamic-update-slice_fusion.3
  204.9 1.1 constant_dynamic-update-slice_fusion.2
  206.0 1.1 constant_dynamic-update-slice_fusion.1
  207.1 5.5 %collective-permute-done.14 = f32[1,16,128,128]{3,2,1,0:T(8,128)S(1)} collective-permute-done((f32[1,16,128,128]{3,2,1,0:T(8,128)S(1)}, f32[1,16,128,128]{3,2,1,0:T(8,128)S(1)}, u32[]{:S(2)}, u32[]{:S(2)}) %collective-permute-start.14) | collective-permute-done | bytes 1048608 | tf_op jit(solution)/shard_map/ppermute | solution.py:43
  212.6 1.2 constant_dynamic-update-slice_fusion
  213.8 7.9 %select_reduce_fusion = bf16[16,128,128]{2,1,0:T(8,128)(2,1)S(1)} fusion(f32[16,16,128,128]{3,2,1,0:T(8,128)} %constant_dynamic-update-slice_fusion, pred[16]{0:T(512)(128)(4,1)S(1)} %iota_compare_fusion.3), kind=kLoop, calls=%fused_computation.3 | loop fusion | flops 8126464 | bytes 17301520 | tf_op jit(solution)/shard_map/reduce_sum | solution.py:55
  221.8 2.3 multiply_reduce_fusion.1
  224.1 0.2 broadcast_multiply_fusion
  224.3 1.8 copy.40
  226.1 2.1 fusion.24
  228.2 1.3 fusion.26
  229.5 23.3 %scatter_custom_fusion = bf16[1536,2048]{1,0:T(8,128)(2,1)} fusion(s32[1024]{0:T(1024)S(1)} %bitcast.123, bf16[256,2048]{1,0:T(8,128)(2,1)} %fusion.26, s32[1024]{0:T(1024)S(1)} %broadcast_clamp_fusion.1, bf16[]{:T(256)} %constant.144.clone.1), kind=kCustom, calls=%fused_computation.20 | custom fusion | bytes 6291968 | tf_op jit(solution)/shard_map/scatter | solution.py:84
  252.8 82.9 %all_to_all.10 = bf16[8,192,2048]{2,1,0:T(8,128)(2,1)S(1)} all-to-all(bf16[8,192,2048]{2,1,0:T(8,128)(2,1)} %bitcast.110), channel_id=1, replica_groups=mesh['seq'=16,'exp'=8] {'exp'}, dimensions={0} | all-to-all | bytes 12582912 | tf_op jit(solution)/shard_map/all_to_all | solution.py:89
  335.7 2.6 copy-done.1
  338.3 13.4 %fusion.6 = f32[8,192,1408]{2,1,0:T(8,128)} fusion(bf16[8,192,2048]{2,1,0:T(8,128)(2,1)S(1)} %all_to_all.10, bf16[1,2048,1408]{2,1,0:T(8,128)(2,1)} %param.20), kind=kOutput, calls=%fused_computation.14 | convolution fusion | flops 8858370048 | bytes 20709376 | tf_op jit(solution)/shard_map/gend,edf->genf/dot_general | solution.py:93
  351.7 28.7 %fusion.9 = bf16[8,192,2048]{2,1,0:T(8,128)(2,1)} fusion(bf16[1,1408,2048]{2,1,0:T(8,128)(2,1)} %param.21, f32[8,192,1408]{2,1,0:T(8,128)} %fusion.6, bf16[8,192,2048]{2,1,0:T(8,128)(2,1)} %copy-done.1, bf16[1,2048,1408]{2,1,0:T(8,128)(2,1)} %param.19), kind=kOutput, calls=%fused_computation.17 | convolution fusion | flops 17732861952 | bytes 32768000 | tf_op jit(solution)/shard_map/genf,efd->gend/dot_general | solution.py:95
  380.4 6.0 %all-to-all-start.1 = ((bf16[8,192,2048]{2,1,0:T(8,128)(2,1)}), bf16[8,192,2048]{2,1,0:T(8,128)(2,1)}, u32[]{:S(2)}, u32[]{:S(2)}) async-start(bf16[8,192,2048]{2,1,0:T(8,128)(2,1)} %fusion.9), calls=%async_computation.1 | async-start | bytes 12582912 | tf_op jit(solution)/shard_map/all_to_all | solution.py:97
  386.4 0.1 copy.41
  386.6 1.8 copy.36
  388.4 69.2 %all-to-all-done.1 = bf16[8,192,2048]{2,1,0:T(8,128)(2,1)} async-done(((bf16[8,192,2048]{2,1,0:T(8,128)(2,1)}), bf16[8,192,2048]{2,1,0:T(8,128)(2,1)}, u32[]{:S(2)}, u32[]{:S(2)}) %all-to-all-start.1) | async-done | bytes 6291488 | tf_op jit(solution)/shard_map/all_to_all | solution.py:97
  457.6 12.4 %gather_fusion = bf16[1024,2048]{1,0:T(8,128)(2,1)} fusion(bf16[1536,2048]{1,0:T(8,128)(2,1)} %bitcast.26, s32[1024]{0:T(1024)S(1)} %broadcast_clamp_fusion), kind=kCustom, calls=%fused_computation.1 | custom fusion | bytes 8392704 | tf_op jit(solution)/shard_map/gather | solution.py:98
  470.0 8.3 %reshape.198 = f32[256,4,2048]{2,1,0:T(4,128)} reshape(bf16[1024,2048]{1,0:T(8,128)(2,1)} %gather_fusion) | data formatting | bytes 12582912 | tf_op jit(solution)/shard_map/convert_element_type | solution.py:99
  478.3 11.5 %multiply_reduce_fusion = f32[256,2048]{1,0:T(8,128)} fusion(f32[256,4,2048]{2,1,0:T(4,128)} %reshape.198, f32[256,4]{1,0:T(8,128)S(1)} %copy.41), kind=kLoop, calls=%fused_computation.11 | loop fusion | flops 3670016 | bytes 10489856 | tf_op jit(solution)/shard_map/reduce_sum | solution.py:99
  489.8 3.1 fusion.27
  (60 shorter events, 0.5 us)
Async XLA Ops:
  2.9 117.0 %copy-start.15 = (s32[1,256,4]{1,2,0:T(4,128)S(1)}, s32[1,256,4]{1,2,0:T(4,128)}, u32[]{:S(2)}) copy-start(s32[1,256,4]{1,2,0:T(4,128)} %param.17) | copy-start | bytes 12292
  12.3 29.6 %collective-permute-start = (f32[1,16,128,128]{3,2,1,0:T(8,128)S(1)}, f32[1,16,128,128]{3,2,1,0:T(8,128)S(1)}, u32[]{:S(2)}, u32[]{:S(2)}) collective-permute-start(f32[1,16,128,128]{3,2,1,0:T(8,128)S(1)} %get-tuple-element.8), channel_id=1, source_target_pairs={{0,8},{8,16},{16,24},{24,32},{32,40},{40,48},{48,56},{56,64},{64,7... | collective-permute-start | bytes 3145736 | tf_op jit(solution)/shard_map/ppermute | solution.py:43
  14.3 27.6 %collective-permute-start.1 = (f32[1,16,128,128]{3,2,1,0:T(8,128)S(1)}, f32[1,16,128,128]{3,2,1,0:T(8,128)S(1)}, u32[]{:S(2)}, u32[]{:S(2)}) collective-permute-start(f32[1,16,128,128]{3,2,1,0:T(8,128)S(1)} %get-tuple-element.8), channel_id=1, source_target_pairs={{0,120},{8,0},{16,8},{24,16},{32,24},{40,32},{48,40},{56,48},{64,5... | collective-permute-start | bytes 3145736 | tf_op jit(solution)/shard_map/ppermute | solution.py:48
  41.9 77.9 %copy-start.5 = (f32[1,16,128,128]{3,2,1,0:T(8,128)}, f32[1,16,128,128]{3,2,1,0:T(8,128)S(1)}, u32[]{:S(2)}) copy-start(f32[1,16,128,128]{3,2,1,0:T(8,128)S(1)} %collective-permute-done) | copy-start | bytes 3145732
  41.9 26.8 %collective-permute-start.2 = (f32[1,16,128,128]{3,2,1,0:T(8,128)S(1)}, f32[1,16,128,128]{3,2,1,0:T(8,128)S(1)}, u32[]{:S(2)}, u32[]{:S(2)}) collective-permute-start(f32[1,16,128,128]{3,2,1,0:T(8,128)S(1)} %collective-permute-done), channel_id=1, source_target_pairs={{0,8},{8,16},{16,24},{24,32},{32,40},{40,48},{48,56},{56,64},{64,7... | collective-permute-start | bytes 3145736 | tf_op jit(solution)/shard_map/ppermute | solution.py:43
  41.9 77.9 %copy-start.6 = (f32[1,16,128,128]{3,2,1,0:T(8,128)}, f32[1,16,128,128]{3,2,1,0:T(8,128)S(1)}, u32[]{:S(2)}) copy-start(f32[1,16,128,128]{3,2,1,0:T(8,128)S(1)} %collective-permute-done.1) | copy-start | bytes 3145732
  41.9 26.8 %collective-permute-start.3 = (f32[1,16,128,128]{3,2,1,0:T(8,128)S(1)}, f32[1,16,128,128]{3,2,1,0:T(8,128)S(1)}, u32[]{:S(2)}, u32[]{:S(2)}) collective-permute-start(f32[1,16,128,128]{3,2,1,0:T(8,128)S(1)} %collective-permute-done.1), channel_id=1, source_target_pairs={{0,120},{8,0},{16,8},{24,16},{32,24},{40,32},{48,40},{56,48},{64,5... | collective-permute-start | bytes 3145736 | tf_op jit(solution)/shard_map/ppermute | solution.py:48
  68.7 51.1 %copy-start.7 = (f32[1,16,128,128]{3,2,1,0:T(8,128)}, f32[1,16,128,128]{3,2,1,0:T(8,128)S(1)}, u32[]{:S(2)}) copy-start(f32[1,16,128,128]{3,2,1,0:T(8,128)S(1)} %collective-permute-done.2) | copy-start | bytes 3145732
  68.7 25.9 %collective-permute-start.4 = (f32[1,16,128,128]{3,2,1,0:T(8,128)S(1)}, f32[1,16,128,128]{3,2,1,0:T(8,128)S(1)}, u32[]{:S(2)}, u32[]{:S(2)}) collective-permute-start(f32[1,16,128,128]{3,2,1,0:T(8,128)S(1)} %collective-permute-done.2), channel_id=1, source_target_pairs={{0,8},{8,16},{16,24},{24,32},{32,40},{40,48},{48,56},{56,64},{64,7... | collective-permute-start | bytes 3145736 | tf_op jit(solution)/shard_map/ppermute | solution.py:43
  68.7 51.1 %copy-start.10 = (f32[1,16,128,128]{3,2,1,0:T(8,128)}, f32[1,16,128,128]{3,2,1,0:T(8,128)S(1)}, u32[]{:S(2)}) copy-start(f32[1,16,128,128]{3,2,1,0:T(8,128)S(1)} %collective-permute-done.3) | copy-start | bytes 3145732
  68.7 25.9 %collective-permute-start.5 = (f32[1,16,128,128]{3,2,1,0:T(8,128)S(1)}, f32[1,16,128,128]{3,2,1,0:T(8,128)S(1)}, u32[]{:S(2)}, u32[]{:S(2)}) collective-permute-start(f32[1,16,128,128]{3,2,1,0:T(8,128)S(1)} %collective-permute-done.3), channel_id=1, source_target_pairs={{0,120},{8,0},{16,8},{24,16},{32,24},{40,32},{48,40},{56,48},{64,5... | collective-permute-start | bytes 3145736 | tf_op jit(solution)/shard_map/ppermute | solution.py:48
  94.6 25.2 %copy-start.12 = (f32[1,16,128,128]{3,2,1,0:T(8,128)}, f32[1,16,128,128]{3,2,1,0:T(8,128)S(1)}, u32[]{:S(2)}) copy-start(f32[1,16,128,128]{3,2,1,0:T(8,128)S(1)} %collective-permute-done.4) | copy-start | bytes 3145732
  94.6 25.2 %collective-permute-start.6 = (f32[1,16,128,128]{3,2,1,0:T(8,128)S(1)}, f32[1,16,128,128]{3,2,1,0:T(8,128)}, u32[]{:S(2)}, u32[]{:S(2)}) collective-permute-start(f32[1,16,128,128]{3,2,1,0:T(8,128)S(1)} %collective-permute-done.4), channel_id=1, source_target_pairs={{0,8},{8,16},{16,24},{24,32},{32,40},{40,48},{48,56},{56,64},{64,7... | collective-permute-start | bytes 3145736 | tf_op jit(solution)/shard_map/ppermute | solution.py:43
  94.6 33.1 %copy-start.8 = (f32[1,16,128,128]{3,2,1,0:T(8,128)}, f32[1,16,128,128]{3,2,1,0:T(8,128)S(1)}, u32[]{:S(2)}) copy-start(f32[1,16,128,128]{3,2,1,0:T(8,128)S(1)} %collective-permute-done.5) | copy-start | bytes 3145732
  94.6 27.8 %collective-permute-start.7 = (f32[1,16,128,128]{3,2,1,0:T(8,128)S(1)}, f32[1,16,128,128]{3,2,1,0:T(8,128)}, u32[]{:S(2)}, u32[]{:S(2)}) collective-permute-start(f32[1,16,128,128]{3,2,1,0:T(8,128)S(1)} %collective-permute-done.5), channel_id=1, source_target_pairs={{0,120},{8,0},{16,8},{24,16},{32,24},{40,32},{48,40},{56,48},{64,5... | collective-permute-start | bytes 3145736 | tf_op jit(solution)/shard_map/ppermute | solution.py:48
  119.8 24.6 %collective-permute-start.8 = (f32[1,16,128,128]{3,2,1,0:T(8,128)}, f32[1,16,128,128]{3,2,1,0:T(8,128)}, u32[]{:S(2)}, u32[]{:S(2)}) collective-permute-start(f32[1,16,128,128]{3,2,1,0:T(8,128)} %collective-permute-done.6), channel_id=1, source_target_pairs={{0,8},{8,16},{16,24},{24,32},{32,40},{40,48},{48,56},{56,64},{64,7... | collective-permute-start | bytes 3145736 | tf_op jit(solution)/shard_map/ppermute | solution.py:43
  122.5 24.8 %collective-permute-start.9 = (f32[1,16,128,128]{3,2,1,0:T(8,128)}, f32[1,16,128,128]{3,2,1,0:T(8,128)}, u32[]{:S(2)}, u32[]{:S(2)}) collective-permute-start(f32[1,16,128,128]{3,2,1,0:T(8,128)} %collective-permute-done.7), channel_id=1, source_target_pairs={{0,120},{8,0},{16,8},{24,16},{32,24},{40,32},{48,40},{56,48},{64,5... | collective-permute-start | bytes 3145736 | tf_op jit(solution)/shard_map/ppermute | solution.py:48
  129.1 45.9 %copy-start.3 = (bf16[32,8,16,128]{3,2,1,0:T(8,128)(2,1)}, bf16[32,8,16,128]{3,2,1,0:T(8,128)(2,1)S(1)}, u32[]{:S(2)}) copy-start(bf16[32,8,16,128]{3,2,1,0:T(8,128)(2,1)S(1)} %copy.44) | copy-start | bytes 3145732
  144.4 23.7 %collective-permute-start.10 = (f32[1,16,128,128]{3,2,1,0:T(8,128)}, f32[1,16,128,128]{3,2,1,0:T(8,128)}, u32[]{:S(2)}, u32[]{:S(2)}) collective-permute-start(f32[1,16,128,128]{3,2,1,0:T(8,128)} %collective-permute-done.8), channel_id=1, source_target_pairs={{0,8},{8,16},{16,24},{24,32},{32,40},{40,48},{48,56},{56,64},{64,7... | collective-permute-start | bytes 3145736 | tf_op jit(solution)/shard_map/ppermute | solution.py:43
  147.2 27.8 %copy-start.11 = (f32[1,16,128,128]{3,2,1,0:T(8,128)S(1)}, f32[1,16,128,128]{3,2,1,0:T(8,128)}, u32[]{:S(2)}) copy-start(f32[1,16,128,128]{3,2,1,0:T(8,128)} %copy-done.10) | copy-start | bytes 3145732
  147.2 34.8 %copy-start.9 = (f32[1,16,128,128]{3,2,1,0:T(8,128)S(1)}, f32[1,16,128,128]{3,2,1,0:T(8,128)}, u32[]{:S(2)}) copy-start(f32[1,16,128,128]{3,2,1,0:T(8,128)} %copy-done.8) | copy-start | bytes 3145732
  147.2 30.0 %collective-permute-start.11 = (f32[1,16,128,128]{3,2,1,0:T(8,128)}, f32[1,16,128,128]{3,2,1,0:T(8,128)}, u32[]{:S(2)}, u32[]{:S(2)}) collective-permute-start(f32[1,16,128,128]{3,2,1,0:T(8,128)} %collective-permute-done.9), channel_id=1, source_target_pairs={{0,120},{8,0},{16,8},{24,16},{32,24},{40,32},{48,40},{56,48},{64,5... | collective-permute-start | bytes 3145736 | tf_op jit(solution)/shard_map/ppermute | solution.py:48
  152.3 23.8 %copy-start.13 = (f32[1,16,128,128]{3,2,1,0:T(8,128)S(1)}, f32[1,16,128,128]{3,2,1,0:T(8,128)}, u32[]{:S(2)}) copy-start(f32[1,16,128,128]{3,2,1,0:T(8,128)} %copy-done.12) | copy-start | bytes 3145732
  168.1 22.7 %collective-permute-start.12 = (f32[1,16,128,128]{3,2,1,0:T(8,128)}, f32[1,16,128,128]{3,2,1,0:T(8,128)S(1)}, u32[]{:S(2)}, u32[]{:S(2)}) collective-permute-start(f32[1,16,128,128]{3,2,1,0:T(8,128)} %collective-permute-done.10), channel_id=1, source_target_pairs={{0,8},{8,16},{16,24},{24,32},{32,40},{40,48},{48,56},{56,64},{64,7... | collective-permute-start | bytes 3145736 | tf_op jit(solution)/shard_map/ppermute | solution.py:43
  177.2 28.8 %collective-permute-start.13 = (f32[1,16,128,128]{3,2,1,0:T(8,128)}, f32[1,16,128,128]{3,2,1,0:T(8,128)S(1)}, u32[]{:S(2)}, u32[]{:S(2)}) collective-permute-start(f32[1,16,128,128]{3,2,1,0:T(8,128)} %collective-permute-done.11), channel_id=1, source_target_pairs={{0,120},{8,0},{16,8},{24,16},{32,24},{40,32},{48,40},{56,48},{64,5... | collective-permute-start | bytes 3145736 | tf_op jit(solution)/shard_map/ppermute | solution.py:48
  190.8 21.8 %collective-permute-start.14 = (f32[1,16,128,128]{3,2,1,0:T(8,128)S(1)}, f32[1,16,128,128]{3,2,1,0:T(8,128)S(1)}, u32[]{:S(2)}, u32[]{:S(2)}) collective-permute-start(f32[1,16,128,128]{3,2,1,0:T(8,128)S(1)} %collective-permute-done.12), channel_id=1, source_target_pairs={{0,8},{8,16},{16,24},{24,32},{32,40},{40,48},{48,56},{56,64},{64,7... | collective-permute-start | bytes 3145736 | tf_op jit(solution)/shard_map/ppermute | solution.py:43
  213.8 8.0 %copy-start.4 = (bf16[32,8,16,128]{3,2,1,0:T(8,128)(2,1)S(1)}, bf16[32,8,16,128]{3,2,1,0:T(8,128)(2,1)}, u32[]{:S(2)}) copy-start(bf16[32,8,16,128]{3,2,1,0:T(8,128)(2,1)} %copy-done.3) | copy-start | bytes 3145732
  221.7 4.4 copy-start.2
  221.8 4.4 copy-start.14
  224.0 4.2 copy-start.16
  335.7 2.6 copy-start.1
  380.4 6.0 %copy-start.17 = (f32[1,256,4]{1,2,0:T(4,128)S(1)}, f32[1,256,4]{1,2,0:T(4,128)}, u32[]{:S(2)}) copy-start(f32[1,256,4]{1,2,0:T(4,128)} %param.18) | copy-start | bytes 12292
  380.4 77.2 %all-to-all-start.1 = ((bf16[8,192,2048]{2,1,0:T(8,128)(2,1)}), bf16[8,192,2048]{2,1,0:T(8,128)(2,1)}, u32[]{:S(2)}, u32[]{:S(2)}) async-start(bf16[8,192,2048]{2,1,0:T(8,128)(2,1)} %fusion.9), calls=%async_computation.1 | async-start | bytes 12582912 | tf_op jit(solution)/shard_map/all_to_all | solution.py:97
  478.3 11.5 %copy-start = (f32[1,256,2048]{2,1,0:T(8,128)S(1)}, f32[1,256,2048]{2,1,0:T(8,128)}, u32[]{:S(2)}) copy-start(f32[1,256,2048]{2,1,0:T(8,128)} %copy.36) | copy-start | bytes 6291460
